TPU v7x, 256 devices: a whole 4x4x8 slice. The times are simulated.
256 devices in a mesh: dp: 4 (over y), head: 4 (over x), seq: 16 (over z, core).
Axes of the slice: x: 4, y: 4, z: 8, core: 2. Of those that a mesh axis runs over, the one named last changes fastest.
Arguments:
- q_dense: bfloat16 [32768, 8, 128], P(('dp', 'seq'), 'head'), parts along dimension 0, may hold values from -108 to 108
- k_dense: bfloat16 [32768, 8, 128], P(('dp', 'seq'), 'head'), parts along dimension 0, may hold values from -4 to 4
- v_dense: bfloat16 [32768, 8, 128], P(('dp', 'seq'), 'head'), parts along dimension 0, may hold values from -4 to 4
- q_expert: bfloat16 [32768, 12, 128], P(('dp', 'seq'), 'head'), parts along dimension 0, may hold values from -108 to 108
- k_expert: bfloat16 [32768, 12, 128], P(('dp', 'seq'), 'head'), parts along dimension 0, may hold values from -4 to 4
- v_expert: bfloat16 [32768, 12, 128], P(('dp', 'seq'), 'head'), parts along dimension 0, may hold values from -4 to 4
- gate_logit: bfloat16 [12, 32768], P('head', ('dp', 'seq')), parts along dimension 1, may hold values from -8 to 8
- selection: int32 [12, 2048], P('head', 'dp'), parts along dimension 1, may hold values from 0 to 8191, as said below
Outputs:
- dense_out: bfloat16 [32768, 8, 128], P(('dp', 'seq'), 'head'), parts along dimension 0
- expert_out: bfloat16 [32768, 12, 128], P(('dp', 'seq'), 'head'), parts along dimension 0
There are 4 independent parts, one for each index of `dp`. A program takes and returns all parts, laid end to end along the dimension named above; each array names one. Nothing has to cross between parts.
Inputs may be any that keep to these rules, and one draw needn't show every extreme that they name: `selection`: each row lists 512 distinct token positions in increasing order; every row holds the first and the last token.
All inputs are finite; a program needn't handle non-finite values.
Results may differ from a plain program's by a relative error of at most 0.0055.
Values may be sent and summed in bfloat16 or wider, within the bound.
No kernel may reach another device: no remote copies, remote signals or barrier semaphores. Data moves between devices by JAX's collectives and lax.ppermute only.
A program may use at most 64 MiB of HBM per device.

v0:
```python
import math
import jax
import jax.numpy as jnp
from jax import lax
from jax.sharding import PartitionSpec as P

NEGATIVE = -1e30


def plain_rows(rows, tok_rows, count):
    return rows


def online_update(state, queries, query_pos, keys, values, key_pos, scale):
    leading, total, summed = state
    scores = jnp.einsum("qhd,khd->qhk", queries, keys, preferred_element_type=jnp.float32) * scale
    visible = key_pos[None, None, :] <= query_pos[:, None, None]
    scores = jnp.where(visible, scores, NEGATIVE)
    new_leading = jnp.maximum(leading, jnp.max(scores, axis=2))
    shrink = jnp.exp(leading - new_leading)
    weights = jnp.where(visible, jnp.exp(scores - new_leading[:, :, None]), 0.0)
    total = total * shrink + jnp.sum(weights, axis=2)
    moved = jnp.einsum(
        "qhk,khd->qhd", weights.astype(jnp.bfloat16), values, preferred_element_type=jnp.float32
    )
    return (new_leading, total, summed * shrink[:, :, None] + moved)


def dense_heads(queries, keys, values, position_map):
    tok_rows, heads, width = queries.shape
    count = lax.axis_size("seq")
    half_rows = tok_rows // 2
    own_rows = lax.axis_index("seq") * tok_rows + jnp.arange(tok_rows, dtype=jnp.int32)
    query_pos = position_map(own_rows, tok_rows, count).reshape(2, half_rows)
    groups = queries.reshape(2, half_rows, heads, width)
    scale = 1.0 / math.sqrt(width)
    blank = (
        jnp.full((half_rows, heads), NEGATIVE, jnp.float32),
        jnp.zeros((half_rows, heads), jnp.float32),
        jnp.zeros((half_rows, heads, width), jnp.float32),
    )
    key_rows = lax.all_gather(keys, "seq", axis=0, tiled=True)
    value_rows = lax.all_gather(values, "seq", axis=0, tiled=True)
    length = key_rows.shape[0]
    block = math.gcd(length, 512)
    count_blocks = length // block
    key_pos = position_map(jnp.arange(length, dtype=jnp.int32), tok_rows, count).reshape(
        count_blocks, block
    )
    key_blocks = key_rows.reshape(count_blocks, block, heads, width)
    value_blocks = value_rows.reshape(count_blocks, block, heads, width)

    def advance(state, item):
        key_block, value_block, block_pos = item
        result = []
        for group in range(2):
            seen = jnp.min(block_pos) <= jnp.max(query_pos[group])
            result.append(
                lax.cond(
                    seen,
                    lambda inner, member=group: online_update(
                        inner,
                        groups[member],
                        query_pos[member],
                        key_block,
                        value_block,
                        block_pos,
                        scale,
                    ),
                    lambda inner: inner,
                    state[group],
                )
            )
        return (tuple(result), None)

    final_state, unused = lax.scan(advance, (blank, blank), (key_blocks, value_blocks, key_pos))
    outputs = [
        (summed / total[:, :, None]).astype(jnp.bfloat16) for leading, total, summed in final_state
    ]
    return jnp.concatenate(outputs, axis=0)


def attend_ranked(query_rows, query_ranks, keys, values, gate_rows):
    heads, rows, width = query_rows.shape
    block = math.gcd(rows, 512)
    scale = 1.0 / math.sqrt(width)
    key_ranks = jnp.arange(keys.shape[1], dtype=jnp.int32)

    def one_block(index):
        scores = (
            jnp.einsum("erd,ekd->erk", query_rows, keys, preferred_element_type=jnp.float32) * scale
        )
        visible = key_ranks[None, None, :] <= query_ranks[:, :, None]
        scores = jnp.where(visible, scores, NEGATIVE)
        leading = jnp.max(scores, axis=2, keepdims=True)
        weights = jnp.where(visible, jnp.exp(scores - leading), 0.0)
        total = jnp.sum(weights, axis=2, keepdims=True)
        mixed = (
            jnp.einsum(
                "erk,ekd->erd",
                weights.astype(jnp.bfloat16),
                values,
                preferred_element_type=jnp.float32,
            )
            / total
        )
        return (mixed * jax.nn.sigmoid(gate_rows.astype(jnp.float32))[:, :, None]).astype(
            jnp.bfloat16
        )

    blocks = lax.map(one_block, jnp.arange(rows // block, dtype=jnp.int32))
    return jnp.moveaxis(blocks, 0, 1).reshape(heads, rows, width)


def sparse_heads(queries, keys, values, gate_logit, selection):
    tok_rows, heads, width = queries.shape
    chosen = selection.shape[1]
    start = lax.axis_index("seq") * tok_rows
    positions = start + jnp.arange(tok_rows, dtype=jnp.int32)
    matches = selection[:, :, None] == positions[None, None, :]
    one_hot = matches.astype(jnp.bfloat16)

    def pick(source):
        return jnp.einsum(
            "ent,ted->end", one_hot, source, preferred_element_type=jnp.float32
        ).astype(jnp.bfloat16)

    gate_rows = jnp.einsum("ent,et->en", one_hot, gate_logit, preferred_element_type=jnp.float32)
    gathered = (
        lax.psum(pick(queries), "seq").astype(jnp.float32),
        lax.psum(pick(keys), "seq").astype(jnp.float32),
        lax.psum(pick(values), "seq").astype(jnp.float32),
        lax.psum(gate_rows.astype(jnp.bfloat16), "seq").astype(jnp.float32),
    )
    picked_q, picked_k, picked_v, picked_gate = [member.astype(jnp.bfloat16) for member in gathered]
    all_ranks = jnp.broadcast_to(jnp.arange(chosen, dtype=jnp.int32)[None, :], (heads, chosen))
    results = attend_ranked(picked_q, all_ranks, picked_k, picked_v, picked_gate)
    return jnp.einsum("ent,end->ted", one_hot, results, preferred_element_type=jnp.float32).astype(
        jnp.bfloat16
    )


def local(q_dense, k_dense, v_dense, q_expert, k_expert, v_expert, gate_logit, selection):
    dense_out = dense_heads(q_dense, k_dense, v_dense, plain_rows)
    expert_out = sparse_heads(q_expert, k_expert, v_expert, gate_logit, selection)
    return (dense_out, expert_out)


def solution(mesh):
    placed = (
        P(("dp", "seq"), "head", None),
        P(("dp", "seq"), "head", None),
        P(("dp", "seq"), "head", None),
        P(("dp", "seq"), "head", None),
        P(("dp", "seq"), "head", None),
        P(("dp", "seq"), "head", None),
        P("head", ("dp", "seq")),
        P("head", "dp"),
    )
    return jax.shard_map(
        local,
        mesh=mesh,
        in_specs=placed,
        out_specs=(P(("dp", "seq"), "head", None), P(("dp", "seq"), "head", None)),
        check_vma=False,
    )
```

profile of v0, /device:TPU:225, one launch (start us, length us, event | category | flops | bytes accessed | tf_op | source)
XLA Modules:
  0.0 332.1 jit_solution(16076033150022781153)
XLA Ops:
  8.2 2.1 fusion.67
  10.3 2.5 fusion.61
  12.7 1.4 fusion.64
  16.6 23.1 %psum.31 = bf16[3,512]{1,0:T(4,128)(2,1)S(1)} all-reduce(bf16[3,512]{1,0:T(4,128)(2,1)S(1)} %bitcast.68), channel_id=1, replica_groups=mesh['dp'=4,'head'=4,'seq'=16] {'seq'}, use_global_device_ids=true, to_apply=%region_18.19 | all-reduce | flops 1536 | bytes 6144 | tf_op jit(solution)/shard_map/psum | solution.py:133
  40.3 87.0 %all-reduce.3.cloned.1.call-done = (bf16[3,512,128]{2,1,0:T(8,128)(2,1)}, bf16[3,512,128]{2,1,0:T(8,128)(2,1)}, bf16[3,512,128]{2,1,0:T(8,128)(2,1)}) async-done(((bf16[3,512,128]{2,1,0:T(8,128)(2,1)}, bf16[3,512,128]{2,1,0:T(8,128)(2,1)}, bf16[3,512,128]{2,1,0:T(8,128)(2,1)}), (bf16[3,512,128]{2,1,0:T(8,128)(2,1)}, bf16[3,512,128]{2,1,0:T(8,128)(2,1)}, ...) | async-done | bytes 1179664 | tf_op jit(solution)/shard_map/psum | solution.py:132
  127.3 2.1 fusion.90
  129.5 1.6 fusion.73
  132.0 39.2 %all-gather.3.cloned.1.call-done = bf16[8192,2,128]{2,0,1:T(8,128)(2,1)} async-done(((bf16[512,2,128]{2,0,1:T(8,128)(2,1)}), bf16[8192,2,128]{2,0,1:T(8,128)(2,1)}) %all-gather.3.cloned.1.call-update) | async-done | bytes 4194320 | tf_op jit(solution)/shard_map/all_gather | solution.py:42
  171.2 42.6 %all-gather.5.cloned.1.call-done = bf16[8192,2,128]{2,0,1:T(8,128)(2,1)} async-done(((bf16[512,2,128]{2,0,1:T(8,128)(2,1)}), bf16[8192,2,128]{2,0,1:T(8,128)(2,1)}) %all-gather.5.cloned.1.call-update) | async-done | bytes 4194320 | tf_op jit(solution)/shard_map/all_gather | solution.py:43
  213.9 109.1 %while.26 = (s32[]{:T(128)}, f32[256,2]{0,1:T(2,128)S(1)}, f32[256,2]{0,1:T(2,128)S(1)}, f32[256,2,128]{2,0,1:T(8,128)S(1)}, f32[256,2]{0,1:T(2,128)S(1)}, /*ind...) while((s32[]{:T(128)}, f32[256,2]{0,1:T(2,128)S(1)}, ...), condition=%wide.region_12.13_spmd.clone, body=%wide.region_2.12_spmd.clone.sunk | while | flops 273682432 | bytes 10830257 | solution.py:76
  217.0 1.3 conditional.6
  223.8 1.3 conditional.6
  226.3 1.3 conditional.7
  233.1 1.3 conditional.7
  237.4 1.3 conditional.6
  239.9 1.3 conditional.7
  246.7 1.3 conditional.7
  251.0 1.3 conditional.6
  253.5 1.3 conditional.7
  257.9 1.3 conditional.6
  264.7 1.3 conditional.6
  267.2 1.3 conditional.7
  278.3 1.3 conditional.6
  280.8 1.3 conditional.7
  291.9 1.3 conditional.6
  294.4 1.3 conditional.7
  301.2 1.3 conditional.7
  305.6 1.3 conditional.6
  308.1 1.3 conditional.7
  312.4 1.3 conditional.6
  319.2 1.3 conditional.6
  321.7 1.3 conditional.7
  (357 shorter events, 87.0 us)
Async XLA Ops:
  7.2 1.0 copy-start
  7.2 5.6 %copy-start.6 = (s32[3,512]{1,0:T(4,128)S(1)}, s32[3,512]{1,0:T(4,128)}, u32[]{:S(2)}) copy-start(s32[3,512]{1,0:T(4,128)} %param.21) | copy-start | bytes 18436
  7.2 5.5 %copy-start.4 = (bf16[512,3,128]{2,0,1:T(8,128)(2,1)S(1)}, bf16[512,3,128]{2,0,1:T(8,128)(2,1)}, u32[]{:S(2)}) copy-start(bf16[512,3,128]{2,0,1:T(8,128)(2,1)} %param.18) | copy-start | bytes 1179652
  7.2 120.1 %all-reduce.3.cloned.1.call-start = ((), (), s32[]{:S(2)}) async-start(), calls=%async_computation.2 | async-start | bytes 2359296 | tf_op jit(solution)/shard_map/psum | solution.py:132
  10.3 4.0 %copy-start.1 = (bf16[512,2,128]{2,1,0:T(2,128)(2,1)S(1)}, bf16[512,2,128]{2,1,0:T(2,128)(2,1)}, u32[]{:S(2)}) copy-start(bf16[512,2,128]{2,1,0:T(2,128)(2,1)} %param.15) | copy-start | bytes 786436
  10.3 4.8 %copy-start.2 = (bf16[512,2,128]{2,1,0:T(2,128)(2,1)S(1)}, bf16[512,2,128]{2,1,0:T(2,128)(2,1)}, u32[]{:S(2)}) copy-start(bf16[512,2,128]{2,1,0:T(2,128)(2,1)} %param.16) | copy-start | bytes 786436
  10.3 5.6 %copy-start.3 = (bf16[512,2,128]{2,1,0:T(2,128)(2,1)S(1)}, bf16[512,2,128]{2,1,0:T(2,128)(2,1)}, u32[]{:S(2)}) copy-start(bf16[512,2,128]{2,1,0:T(2,128)(2,1)} %param.14) | copy-start | bytes 786436
  12.7 3.2 copy-start.7
  14.2 157.1 %all-gather.3.cloned.1.call-start = ((), (), s32[]{:S(2)}) async-start(), calls=%async_computation | async-start | bytes 4456448 | tf_op jit(solution)/shard_map/all_gather | solution.py:42
  15.0 198.9 %all-gather.5.cloned.1.call-start = ((), (), s32[]{:S(2)}) async-start(), calls=%async_computation.1 | async-start | bytes 4456448 | tf_op jit(solution)/shard_map/all_gather | solution.py:43
  127.3 2.1 copy-start.5
Sparse Core Ops, SparseCore 0:
  14.3 113.0 all-reduce.2
  129.8 41.4 all-gather.2
  173.1 40.6 all-gather.4
where the time goes:
time: 333 us; the launch traced here: 332 us
  waiting for transfers between devices  169 us (51%)
  loops' own time  42.3 us (13%)
  matrix products  36.9 us (11%)
  other arithmetic  25.7 us (8%)
  blocking collectives  23.1 us (7%)
  local copies, waits for them, and re-layouts  21.1 us (6%)
  between operations  13.9 us (4%)
    psum x1, waiting for transfers between devices, sparse_heads(): lax.psum(pick(values), 'seq').astype(jnp.float32)  87 us
    all_gather x1, waiting for transfers between devices, dense_heads(): value_rows = lax.all_gather(values, 'seq', axis=0, tiled=True)  42.6 us
    another operation x1, loops' own time, dense_heads(): lax.scan(advance, (blank, blank), (key_blocks, value_blocks, key_pos))  40.4 us
    all_gather x1, waiting for transfers between devices, dense_heads(): key_rows = lax.all_gather(keys, 'seq', axis=0, tiled=True)  39.2 us
    psum x1, blocking collectives, sparse_heads(): lax.psum(gate_rows.astype(jnp.bfloat16), 'seq').astype(jnp.float32)  23.1 us
    squeeze x16, local copies, waits for them, and re-layouts, dense_heads(): lax.scan(advance, (blank, blank), (key_blocks, value_blocks, key_pos))  17.2 us
    dot_general x32, matrix products, online_update(): jnp.einsum('qhk,khd->qhd', weights.astype(jnp.bfloat16), values, preferre...  16.5 us
    reduce_min x16, other arithmetic, advance(): seen = jnp.min(block_pos) <= jnp.max(query_pos[group])  10.3 us
  transfers between devices with their start and end apart: 3, of which 3 were waited for; matrix products, arithmetic and copies ran while one was open for 2% of the time, Pallas kernels for 0%

commit v1 on v0

--- a/solution.py
+++ b/solution.py
@@ -40,7 +40,9 @@
         jnp.zeros((half_rows, heads, width), jnp.float32),
     )
     key_rows = lax.all_gather(keys, "seq", axis=0, tiled=True)
-    value_rows = lax.all_gather(values, "seq", axis=0, tiled=True)
+    value_rows = jnp.concatenate(
+        lax.all_to_all(jnp.stack([values] * lax.axis_size("seq")), "seq", 0, 0), axis=0
+    )
     length = key_rows.shape[0]
     block = math.gcd(length, 512)
     count_blocks = length // block

time: 333 us -> 360 us (1.081)
  blocking collectives: 23.1 us -> 113 us
  waiting for transfers between devices: 169 us -> 81.9 us
  local copies, waits for them, and re-layouts: 21.1 us -> 37.2 us
  starting transfers between devices: 0.12 us -> 6.39 us
    psum x1, blocking collectives: 23.1 us -> 113 us  [sparse_heads(): lax.psum(gate_rows.astype(jnp.bfloat16), 'seq').astype(jnp.float32)]
    psum x1, waiting for transfers between devices: 87 us -> 42.6 us  [sparse_heads(): lax.psum(pick(values), 'seq').astype(jnp.float32)]
    all_gather x1 -> x0, waiting for transfers between devices: 42.6 us -> none  [dense_heads(): value_rows = lax.all_gather(values, 'seq', axis=0, tiled=True)]
    squeeze x16 -> x32, local copies, waits for them, and re-layouts: 17.2 us -> 31.1 us  [dense_heads(): lax.scan(advance, (blank, blank), (key_blocks, value_blocks, key_pos))]
    all_to_all x0 -> x1, starting transfers between devices: none -> 6.31 us  [dense_heads(): lax.all_to_all(jnp.stack([values] * lax.axis_size('seq')), 'seq', 0, 0)]
  transfers between devices with their start and end apart: 3 -> 3, of which waited for: 3 -> 2; matrix products, arithmetic and copies ran while one was open for 2% -> 3% of each run, Pallas kernels for 0% -> 0%
where the time goes in v1:
time: 360 us; the launch traced here: 358 us
  blocking collectives  113 us (31%)
  waiting for transfers between devices  81.9 us (23%)
  loops' own time  42.9 us (12%)
  local copies, waits for them, and re-layouts  37.2 us (10%)
  matrix products  36.7 us (10%)
  other arithmetic  25.8 us (7%)
  between operations  14.2 us (4%)
  starting transfers between devices  6.39 us (2%)
    psum x1, blocking collectives, sparse_heads(): lax.psum(gate_rows.astype(jnp.bfloat16), 'seq').astype(jnp.float32)  113 us
    psum x1, waiting for transfers between devices, sparse_heads(): lax.psum(pick(values), 'seq').astype(jnp.float32)  42.6 us
    another operation x1, loops' own time, dense_heads(): lax.scan(advance, (blank, blank), (key_blocks, value_blocks, key_pos))  41 us
    all_gather x1, waiting for transfers between devices, dense_heads(): key_rows = lax.all_gather(keys, 'seq', axis=0, tiled=True)  39.3 us
    squeeze x32, local copies, waits for them, and re-layouts, dense_heads(): lax.scan(advance, (blank, blank), (key_blocks, value_blocks, key_pos))  31.1 us
    dot_general x32, matrix products, online_update(): jnp.einsum('qhk,khd->qhd', weights.astype(jnp.bfloat16), values, preferre...  16.3 us
    reduce_min x16, other arithmetic, advance(): seen = jnp.min(block_pos) <= jnp.max(query_pos[group])  10.3 us
    dot_general x32, matrix products, online_update(): jnp.einsum('qhd,khd->qhk', queries, keys, preferred_element_type=jnp.floa...  10.1 us
  transfers between devices with their start and end apart: 3, of which 2 were waited for; matrix products, arithmetic and copies ran while one was open for 3% of the time, Pallas kernels for 0%

profile of v1, /device:TPU:225, one launch (start us, length us, event | category | flops | bytes accessed | tf_op | source)
XLA Modules:
  0.0 358.2 jit_solution(17475764451893710164)
XLA Ops:
  8.2 2.1 fusion.61
  10.2 2.4 fusion.64
  12.7 1.4 fusion.67
  14.2 2.9 stack.2
  17.1 6.3 %all-to-all-start = ((bf16[16,512,2,128]{3,1,2,0:T(8,128)(2,1)}), bf16[16,512,2,128]{3,1,2,0:T(8,128)(2,1)}, u32[]{:S(2)}, u32[]{:S(2)}) async-start(bf16[16,512,2,128]{3,1,2,0:T(8,128)(2,1)} %stack.2), calls=%async_computation | async-start | bytes 8388608 | tf_op jit(solution)/shard_map/all_to_all | solution.py:44
  25.0 113.1 %psum.31 = bf16[3,512]{1,0:T(4,128)(2,1)S(1)} all-reduce(bf16[3,512]{1,0:T(4,128)(2,1)S(1)} %bitcast.66), channel_id=1, replica_groups=mesh['dp'=4,'head'=4,'seq'=16] {'seq'}, use_global_device_ids=true, to_apply=%region_18.19 | all-reduce | flops 1536 | bytes 6144 | tf_op jit(solution)/shard_map/psum | solution.py:135
  138.8 42.6 %all-reduce.3.cloned.1.call-done = (bf16[3,512,128]{2,1,0:T(8,128)(2,1)}, bf16[3,512,128]{2,1,0:T(8,128)(2,1)}, bf16[3,512,128]{2,1,0:T(8,128)(2,1)}) async-done(((bf16[3,512,128]{2,1,0:T(8,128)(2,1)}, bf16[3,512,128]{2,1,0:T(8,128)(2,1)}, bf16[3,512,128]{2,1,0:T(8,128)(2,1)}), (bf16[3,512,128]{2,1,0:T(8,128)(2,1)}, bf16[3,512,128]{2,1,0:T(8,128)(2,1)}, ...) | async-done | bytes 1179664 | tf_op jit(solution)/shard_map/psum | solution.py:134
  181.4 2.1 fusion.90
  183.6 1.6 fusion.73
  186.1 39.3 %all-gather.2.cloned.1.call-done = bf16[8192,2,128]{2,0,1:T(8,128)(2,1)} async-done(((bf16[512,2,128]{2,0,1:T(8,128)(2,1)}), bf16[8192,2,128]{2,0,1:T(8,128)(2,1)}) %all-gather.2.cloned.1.call-update) | async-done | bytes 4194320 | tf_op jit(solution)/shard_map/all_gather | solution.py:42
  225.5 123.4 %while.26 = (s32[]{:T(128)}, f32[256,2]{0,1:T(2,128)S(1)}, f32[256,2]{0,1:T(2,128)S(1)}, f32[256,2,128]{2,0,1:T(8,128)S(1)}, f32[256,2]{0,1:T(2,128)S(1)}, /*ind...) while((s32[]{:T(128)}, f32[256,2]{0,1:T(2,128)S(1)}, ...), condition=%wide.region_12.13_spmd.clone, body=%wide.region_2.12_spmd.clone.sunk | while | flops 273682432 | bytes 10830253 | solution.py:78
  229.3 1.3 conditional.7
  237.1 1.3 conditional.7
  244.8 1.3 conditional.7
  247.3 1.3 conditional.6
  252.5 1.3 conditional.7
  260.2 1.3 conditional.7
  262.7 1.3 conditional.6
  267.9 1.3 conditional.7
  275.6 1.3 conditional.7
  278.2 1.3 conditional.6
  283.3 1.3 conditional.7
  291.0 1.3 conditional.7
  293.6 1.3 conditional.6
  298.7 1.3 conditional.7
  306.4 1.3 conditional.7
  309.0 1.3 conditional.6
  314.2 1.3 conditional.7
  321.9 1.3 conditional.7
  329.6 1.3 conditional.7
  337.3 1.3 conditional.7
  345.0 1.3 conditional.7
  (373 shorter events, 101.2 us)
Async XLA Ops:
  7.2 1.0 copy-start
  7.2 5.5 %copy-start.6 = (s32[3,512]{1,0:T(4,128)S(1)}, s32[3,512]{1,0:T(4,128)}, u32[]{:S(2)}) copy-start(s32[3,512]{1,0:T(4,128)} %param.21) | copy-start | bytes 18436
  7.2 5.5 %copy-start.4 = (bf16[512,3,128]{2,0,1:T(8,128)(2,1)S(1)}, bf16[512,3,128]{2,0,1:T(8,128)(2,1)}, u32[]{:S(2)}) copy-start(bf16[512,3,128]{2,0,1:T(8,128)(2,1)} %param.19) | copy-start | bytes 1179652
  7.2 174.2 %all-reduce.3.cloned.1.call-start = ((), (), s32[]{:S(2)}) async-start(), calls=%async_computation.2 | async-start | bytes 2359296 | tf_op jit(solution)/shard_map/psum | solution.py:134
  10.2 3.9 %copy-start.1 = (bf16[512,2,128]{2,1,0:T(2,128)(2,1)S(1)}, bf16[512,2,128]{2,1,0:T(2,128)(2,1)}, u32[]{:S(2)}) copy-start(bf16[512,2,128]{2,1,0:T(2,128)(2,1)} %param.16) | copy-start | bytes 786436
  17.1 6.4 %copy-start.2 = (bf16[512,2,128]{2,1,0:T(2,128)(2,1)S(1)}, bf16[512,2,128]{2,1,0:T(2,128)(2,1)}, u32[]{:S(2)}) copy-start(bf16[512,2,128]{2,1,0:T(2,128)(2,1)} %param.15) | copy-start | bytes 786436
  17.1 7.1 %copy-start.7 = (bf16[3,512]{1,0:T(4,128)(2,1)S(1)}, bf16[3,512]{1,0:T(4,128)(2,1)}, u32[]{:S(2)}) copy-start(bf16[3,512]{1,0:T(4,128)(2,1)} %param.20) | copy-start | bytes 9220
  17.1 7.8 %copy-start.3 = (bf16[512,2,128]{2,1,0:T(2,128)(2,1)S(1)}, bf16[512,2,128]{2,1,0:T(2,128)(2,1)}, u32[]{:S(2)}) copy-start(bf16[512,2,128]{2,1,0:T(2,128)(2,1)} %param.14) | copy-start | bytes 786436
  17.1 169.0 %all-to-all-start = ((bf16[16,512,2,128]{3,1,2,0:T(8,128)(2,1)}), bf16[16,512,2,128]{3,1,2,0:T(8,128)(2,1)}, u32[]{:S(2)}, u32[]{:S(2)}) async-start(bf16[16,512,2,128]{3,1,2,0:T(8,128)(2,1)} %stack.2), calls=%async_computation | async-start | bytes 8388608 | tf_op jit(solution)/shard_map/all_to_all | solution.py:44
  23.4 202.0 %all-gather.2.cloned.1.call-start = ((), (), s32[]{:S(2)}) async-start(), calls=%async_computation.1 | async-start | bytes 4456448 | tf_op jit(solution)/shard_map/all_gather | solution.py:42
  181.4 2.1 copy-start.5
Sparse Core Ops, SparseCore 0:
  14.2 167.1 all-reduce.2
  183.9 41.4 all-gather.1
